TPU v7x, 32 devices: a whole 2x2x4 slice. The times are simulated.
32 devices in a mesh: groups: 2 (over x), date: 8 (over z, y), row: 2 (over core).
Axes of the slice: x: 2, y: 2, z: 4, core: 2. Of those that a mesh axis runs over, the one named last changes fastest.
Arguments:
- scenes: bfloat16 [16, 4, 512, 1024], P(('groups', 'date'), None, 'row'), parts along dimension 0, may hold values from -6 to 6
- resample_taps: float32 [2, 4, 7], replicated, may hold values from 0 to 0.35
- clear_mask: int32 [16, 128, 8], P('groups', ('row', 'date')), parts along dimension 0, may hold values 0 or 1
Outputs:
- smooth_fine: bfloat16 [16, 4, 512, 1024], P('groups', None, ('row', 'date')), parts along dimension 0
- smooth_half: bfloat16 [16, 4, 256, 512], P('groups', None, ('row', 'date')), parts along dimension 0
- smooth_quarter: bfloat16 [16, 4, 128, 256], P('groups', None, ('row', 'date')), parts along dimension 0
There are 2 independent parts, one for each index of `groups`. A program takes and returns all parts, laid end to end along the dimension named above; an argument that names none is the same for every part. Nothing has to cross between parts.
Inputs may be any that keep to these rules, and one draw needn't show every extreme that they name: `clear_mask`: 1 marks a clear block, 0 a cloudy one.
All inputs are finite; a program needn't handle non-finite values.
Results may differ from a plain program's by a relative error of at most 0.005.
Values may be sent and summed in bfloat16 or wider, within the bound.
No kernel may reach another device: no remote copies, remote signals or barrier semaphores. Data moves between devices by JAX's collectives and lax.ppermute only.
A program may use at most 128 MiB of HBM per device.

v0:
```python
import math
import jax
import jax.numpy as jnp
import numpy as np
from jax import lax
from jax.sharding import PartitionSpec as P

gap_weights = [math.exp(-((k - 4) ** 2) / 8.0) for k in range(9)]
savgol_coeffs = [c / 231.0 for c in [-21.0, 14.0, 39.0, 54.0, 59.0, 54.0, 39.0, 14.0, -21.0]]
pyramid_filter = [0.125, 0.375, 0.375, 0.125]


def padded(block, sides, width):
    for axis, dim in sides:
        count = lax.axis_size(axis)
        forward = [(i, i + 1) for i in range(count - 1)]
        backward = [(target, source) for source, target in forward]
        low = lax.ppermute(
            lax.slice_in_dim(block, block.shape[dim] - width, None, axis=dim), axis, forward
        )
        high = lax.ppermute(lax.slice_in_dim(block, 0, width, axis=dim), axis, backward)
        block = jnp.concatenate([low, block, high], axis=dim)
    return block


def column_taps(values, taps):
    width = values.shape[-1]
    wide = jnp.pad(values, ((0, 0), (0, 0), (3, 3)))
    total = taps[0] * wide[..., 0:width]
    for k in range(1, 7):
        total = total + taps[k] * wide[..., k : k + width]
    return total


def row_taps(values, taps):
    count = values.shape[1] - 6
    total = taps[0] * values[:, 0:count]
    for k in range(1, 7):
        total = total + taps[k] * values[:, k : k + count]
    return total


def halve_table(width):
    source = np.arange(width)[:, None]
    target = np.arange(width // 2)[None, :]
    place = source - 2 * target + 1
    table = np.zeros((width, width // 2), np.float32)
    for p in range(4):
        table = table + pyramid_filter[p] * (place == p)
    return jnp.asarray(table, jnp.bfloat16)


def halve_columns(values):
    table = halve_table(values.shape[-1])
    high = values.astype(jnp.bfloat16)
    low = (values - high.astype(jnp.float32)).astype(jnp.bfloat16)
    dims = (((values.ndim - 1,), (0,)), ((), ()))
    return lax.dot_general(high, table, dims, preferred_element_type=jnp.float32) + lax.dot_general(
        low, table, dims, preferred_element_type=jnp.float32
    )


def halve_rows(extended):
    pairs_count = extended.shape[1] // 2
    pairs = extended.reshape(extended.shape[:1] + (pairs_count, 2) + extended.shape[2:])
    even = pairs[:, :, 0]
    odd = pairs[:, :, 1]
    return (
        pyramid_filter[0] * even[:, :-1]
        + pyramid_filter[1] * odd[:, :-1]
        + pyramid_filter[2] * even[:, 1:]
        + pyramid_filter[3] * odd[:, 1:]
    )


def decimate_rim(extended):
    return halve_columns(halve_rows(extended))


def keep_rows(values, first, total):
    places = first + lax.iota(jnp.int32, values.shape[1])
    inside = (places >= 0) & (places < total)
    return jnp.where(inside[None, :, None], values, 0.0)


def smooth_operator(dates):
    clamp = np.zeros((dates, dates), np.float64)
    near = np.zeros((dates, dates), np.float64)
    for t in range(dates):
        for k in range(9):
            clamp[t, min(max(t + k - 4, 0), dates - 1)] += savgol_coeffs[k]
            if 0 <= t + k - 4 < dates:
                near[t, t + k - 4] = gap_weights[k]
    return (clamp.astype(np.float32), near.astype(np.float32))


def smooth_coefficients(clear):
    dates = clear.shape[0]
    clamp, near = smooth_operator(dates)
    weight = 0.1 + 0.9 * clear
    denom = jnp.einsum("su,uxy->sxy", near, weight, precision=lax.Precision.HIGHEST)
    gap = (1.0 - clear) / denom
    fill = near[:, :, None, None] * weight[None, :] * gap[:, None]
    fill = fill + jnp.eye(dates, dtype=jnp.float32)[:, :, None, None] * clear[None, :]
    return jnp.einsum("ts,suxy->tuxy", clamp, fill, precision=lax.Precision.HIGHEST)


def expand(coeff, rows, cols):
    lead = coeff.shape[:-2]
    rm, cm = coeff.shape[-2:]
    grown = jnp.broadcast_to(coeff[..., :, None, :, None], lead + (rm, rows, cm, cols))
    return grown.reshape(lead + (rm * rows, cm * cols))


def smooth(level, coeff, rows, cols):
    values = level.astype(jnp.float32)
    grown = expand(coeff, rows, cols)
    return jnp.sum(grown * values[None], axis=1).astype(jnp.bfloat16)


def local(scenes, resample_taps, clear_mask):
    rows = scenes.shape[2]
    bands = scenes.shape[1]
    band_index = lax.axis_index("row")
    total_rows = rows * lax.axis_size("row")
    ndate = lax.axis_size("date")
    extended = padded(scenes, (("row", 2),), 6)
    clear = clear_mask.astype(jnp.float32)
    coeff = smooth_coefficients(clear)
    mask_rows = clear.shape[1]
    mask_cols = clear.shape[2]
    fine_rows = rows // ndate
    width = scenes.shape[3]
    fine = []
    half = []
    quarter = []
    for b in range(bands):
        source = extended[:, b].astype(jnp.float32)
        across = column_taps(source, resample_taps[0, b])
        resampled_wide = row_taps(across, resample_taps[1, b])
        resampled_wide = keep_rows(resampled_wide, band_index * rows - 3, total_rows)
        half_wide = decimate_rim(resampled_wide)
        half_wide = keep_rows(half_wide, band_index * (rows // 2) - 1, total_rows // 2)
        level_zero = resampled_wide[:, 3 : 3 + rows].astype(jnp.bfloat16)
        level_one = half_wide[:, 1 : 1 + rows // 2].astype(jnp.bfloat16)
        level_two = decimate_rim(half_wide).astype(jnp.bfloat16)
        got = [
            lax.all_to_all(level, "date", split_axis=1, concat_axis=0, tiled=True)
            for level in (level_zero, level_one, level_two)
        ]
        fine.append(smooth(got[0], coeff, fine_rows // mask_rows, width // mask_cols))
        half.append(smooth(got[1], coeff, fine_rows // 2 // mask_rows, width // 2 // mask_cols))
        quarter.append(smooth(got[2], coeff, fine_rows // 4 // mask_rows, width // 4 // mask_cols))
    return tuple((jnp.stack(parts, axis=1) for parts in (fine, half, quarter)))


def solution(mesh):
    in_specs = (P(("groups", "date"), None, "row", None), P(), P("groups", ("row", "date"), None))
    out_specs = (
        P("groups", None, ("row", "date"), None),
        P("groups", None, ("row", "date"), None),
        P("groups", None, ("row", "date"), None),
    )
    return jax.shard_map(local, mesh=mesh, in_specs=in_specs, out_specs=out_specs, check_vma=False)
```

profile of v0, /device:TPU:0, one launch (start us, length us, event | category | flops | bytes accessed | tf_op | source)
XLA Modules:
  0.0 341.9 jit_solution(5171048793330482264)
XLA Ops:
  1.6 2.4 collective-permute-start
  5.4 1.9 fusion.102
  7.2 1.8 fusion.101
  9.1 1.8 fusion.103
  14.0 5.1 %constant_dynamic-update-slice_fusion.1 = bf16[1,4,268,1024]{3,0,2,1:T(2,128)(2,1)S(1)} fusion(bf16[1,4,268,1024]{3,0,2,1:T(2,128)(2,1)S(1)} %constant_dynamic-update-slice_fusion.2, bf16[1,4,256,1024]{3,2,1,0:T(8,128)(2,1)} %param.14), kind=kLoop, calls=%fused_computation.245 | loop fusion | bytes 6291456
  19.2 5.8 %fusion.12 = (f32[1,268,1024]{2,0,1:T(1,128)S(1)}, f32[1,268,1024]{2,0,1:T(1,128)S(1)}, f32[1,268,1024]{2,0,1:T(1,128)}, f32[1,268,1024]{2,0,1:T(1,128)}) fusion(bf16[1,4,268,1024]{3,0,2,1:T(2,128)(2,1)S(1)} %constant_dynamic-update-slice_fusion), kind=kLoop, calls=%fused_computation.39 | loop fusion | flops 1097728 | bytes 6586368 | tf_op jit(solution)/shard_map/convert_element_type | solution.py:138
  25.0 37.0 %multiply_add_fusion = (f32[1,268,1024]{2,0,1:T(1,128)S(1)}, f32[1,268,1024]{2,0,1:T(1,128)S(1)}) fusion(f32[1,268,1024]{2,0,1:T(1,128)S(1)} %get-tuple-element.31, f32[]{:T(128)} %bitcast.66, f32[]{:T(128)} %bitcast.65, f32[]{:T(128)} %bitcast.64, f32[]{:T(128)} %bitcast.62, f32[]{:T(128)} %bitcast.61, f32[]{:T(128)} %bitcast.60, f32[]{:T(128)} %bitcast.58, ...), kind=kLoop, calls=%fused_computation.46 | loop fusion | flops 7135232 | bytes 4390968 | tf_op jit(solution)/shard_map/add | solution.py:31
  62.0 9.8 %broadcast_select_fusion = f32[1,262,1024]{2,0,1:T(1,128)S(1)} fusion(pred[262]{0:T(512)(128)(4,1)S(1)} %fusion.89, f32[1,268,1024]{2,0,1:T(1,128)S(1)} %get-tuple-element.109, f32[]{:T(128)} %bitcast.72, f32[]{:T(128)} %bitcast.71, f32[]{:T(128)} %bitcast.70, f32[]{:T(128)} %bitcast.69, f32[]{:T(128)} %bitcast.68, f32[]{:T(128)} %bitcast.67, f32[]{:T(128)} %bitcast.57), kind=kLoop, calls=%fused_computation.8 | loop fusion | flops 3756032 | bytes 8585506 | tf_op jit(solution)/shard_map/jit(_where)/select_n | solution.py:83
  72.6 2.1 subtract_convert_fusion
  76.0 2.0 reshape.705
  83.2 7.0 %all-to-all-start.11 = ((bf16[8,2,1024]{2,1,0:T(2,128)(2,1)}), bf16[8,2,1024]{2,1,0:T(2,128)(2,1)}, u32[]{:S(2)}, u32[]{:S(2)}) async-start(bf16[8,2,1024]{2,1,0:T(2,128)(2,1)} %reshape.736), calls=%async_computation.11 | async-start | bytes 65536 | tf_op jit(solution)/shard_map/all_to_all | solution.py:148
  90.2 9.8 %broadcast_select_fusion.1 = f32[1,262,1024]{2,0,1:T(1,128)S(1)} fusion(pred[262]{0:T(512)(128)(4,1)S(1)} %fusion.89, f32[1,268,1024]{2,0,1:T(1,128)S(1)} %get-tuple-element.110, f32[]{:T(128)} %bitcast.54, f32[]{:T(128)} %bitcast.53, f32[]{:T(128)} %bitcast.52, f32[]{:T(128)} %bitcast.51, f32[]{:T(128)} %bitcast.50, f32[]{:T(128)} %bitcast.49, f32[]{:T(128)} %bitcast.39), kind=kLoop, calls=%fused_computation.9 | loop fusion | flops 3756032 | bytes 8585506 | tf_op jit(solution)/shard_map/jit(_where)/select_n | solution.py:83
  100.8 2.1 subtract_convert_fusion.1
  105.2 38.9 %multiply_add_fusion.2 = (f32[1,268,1024]{2,0,1:T(1,128)S(1)}, f32[1,268,1024]{2,0,1:T(1,128)S(1)}) fusion(f32[1,268,1024]{2,0,1:T(1,128)S(1)} %copy-done.8, f32[]{:T(128)} %bitcast.30, f32[]{:T(128)} %bitcast.29, f32[]{:T(128)} %bitcast.28, f32[]{:T(128)} %bitcast.26, f32[]{:T(128)} %bitcast.25, f32[]{:T(128)} %bitcast.24, f32[]{:T(128)} %bitcast.22, ...), kind=kLoop, calls=%fused_computation.52 | loop fusion | flops 7135232 | bytes 4390968 | tf_op jit(solution)/shard_map/add | solution.py:31
  144.2 9.6 %broadcast_select_fusion.2 = f32[1,262,1024]{2,0,1:T(1,128)S(1)} fusion(pred[262]{0:T(512)(128)(4,1)S(1)} %fusion.89, f32[1,268,1024]{2,0,1:T(1,128)S(1)} %get-tuple-element.111, f32[]{:T(128)} %bitcast.36, f32[]{:T(128)} %bitcast.35, f32[]{:T(128)} %bitcast.34, f32[]{:T(128)} %bitcast.33, f32[]{:T(128)} %bitcast.32, f32[]{:T(128)} %bitcast.31, f32[]{:T(128)} %bitcast.21), kind=kLoop, calls=%fused_computation.10 | loop fusion | flops 3756032 | bytes 8585506 | tf_op jit(solution)/shard_map/jit(_where)/select_n | solution.py:83
  154.6 2.1 subtract_convert_fusion.2
  158.0 2.0 reshape.703
  162.9 10.4 %broadcast_select_fusion.3 = f32[1,262,1024]{2,0,1:T(1,128)S(1)} fusion(pred[262]{0:T(512)(128)(4,1)S(1)} %fusion.89, f32[1,268,1024]{2,0,1:T(1,128)S(1)} %get-tuple-element.112, f32[]{:T(128)} %bitcast.18, f32[]{:T(128)} %bitcast.17, f32[]{:T(128)} %bitcast.16, f32[]{:T(128)} %bitcast.15, f32[]{:T(128)} %bitcast.14, f32[]{:T(128)} %bitcast.13, f32[]{:T(128)} %bitcast.3), kind=kLoop, calls=%fused_computation.11 | loop fusion | flops 3756032 | bytes 8585506 | tf_op jit(solution)/shard_map/jit(_where)/select_n | solution.py:83
  174.1 2.1 subtract_convert_fusion.3
  179.4 6.0 %all-to-all-start.10 = ((bf16[8,2,1024]{2,1,0:T(2,128)(2,1)}), bf16[8,2,1024]{2,1,0:T(2,128)(2,1)S(1)}, u32[]{:S(2)}, u32[]{:S(2)}) async-start(bf16[8,2,1024]{2,1,0:T(2,128)(2,1)} %reshape.734), calls=%async_computation.10 | async-start | bytes 65536 | tf_op jit(solution)/shard_map/all_to_all | solution.py:148
  187.0 5.1 %all-to-all-done.10 = bf16[8,2,1024]{2,1,0:T(2,128)(2,1)S(1)} async-done(((bf16[8,2,1024]{2,1,0:T(2,128)(2,1)}), bf16[8,2,1024]{2,1,0:T(2,128)(2,1)S(1)}, u32[]{:S(2)}, u32[]{:S(2)}) %all-to-all-start.10) | async-done | bytes 32800 | tf_op jit(solution)/shard_map/all_to_all | solution.py:148
  192.1 3.3 all-to-all-start.9
  197.1 5.0 %all-to-all-done.9 = bf16[8,2,1024]{2,1,0:T(2,128)(2,1)S(1)} async-done(((bf16[8,2,1024]{2,1,0:T(2,128)(2,1)}), bf16[8,2,1024]{2,1,0:T(2,128)(2,1)S(1)}, u32[]{:S(2)}, u32[]{:S(2)}) %all-to-all-start.9) | async-done | bytes 32800 | tf_op jit(solution)/shard_map/all_to_all | solution.py:148
  202.0 3.3 all-to-all-start.8
  207.8 4.3 %all-to-all-done.8 = bf16[8,2,1024]{2,1,0:T(2,128)(2,1)S(1)} async-done(((bf16[8,2,1024]{2,1,0:T(2,128)(2,1)}), bf16[8,2,1024]{2,1,0:T(2,128)(2,1)S(1)}, u32[]{:S(2)}, u32[]{:S(2)}) %all-to-all-start.8) | async-done | bytes 32800 | tf_op jit(solution)/shard_map/all_to_all | solution.py:148
  212.0 3.4 all-to-all-start.7
  217.8 4.9 %all-to-all-done.7 = bf16[8,2,4096]{2,1,0:T(2,128)(2,1)S(1)} async-done(((bf16[8,2,4096]{2,1,0:T(2,128)(2,1)}), bf16[8,2,4096]{2,1,0:T(2,128)(2,1)S(1)}, u32[]{:S(2)}, u32[]{:S(2)}) %all-to-all-start.7) | async-done | bytes 131104 | tf_op jit(solution)/shard_map/all_to_all | solution.py:148
  222.7 3.4 all-to-all-start.6
  228.4 4.9 %all-to-all-done.6 = bf16[8,2,4096]{2,1,0:T(2,128)(2,1)S(1)} async-done(((bf16[8,2,4096]{2,1,0:T(2,128)(2,1)}), bf16[8,2,4096]{2,1,0:T(2,128)(2,1)S(1)}, u32[]{:S(2)}, u32[]{:S(2)}) %all-to-all-start.6) | async-done | bytes 131104 | tf_op jit(solution)/shard_map/all_to_all | solution.py:148
  233.3 3.4 all-to-all-start.5
  239.1 4.9 %all-to-all-done.5 = bf16[8,2,4096]{2,1,0:T(2,128)(2,1)S(1)} async-done(((bf16[8,2,4096]{2,1,0:T(2,128)(2,1)}), bf16[8,2,4096]{2,1,0:T(2,128)(2,1)S(1)}, u32[]{:S(2)}, u32[]{:S(2)}) %all-to-all-start.5) | async-done | bytes 131104 | tf_op jit(solution)/shard_map/all_to_all | solution.py:148
  244.0 3.5 %all-to-all-start.4 = ((bf16[8,2,4096]{2,1,0:T(2,128)(2,1)}), bf16[8,2,4096]{2,1,0:T(2,128)(2,1)S(1)}, u32[]{:S(2)}, u32[]{:S(2)}) async-start(bf16[8,2,4096]{2,1,0:T(2,128)(2,1)} %reshape.722), calls=%async_computation.4 | async-start | bytes 262144 | tf_op jit(solution)/shard_map/all_to_all | solution.py:148
  248.3 3.6 %reduce.31 = bf16[256,1024]{1,0:T(8,128)(2,1)S(1)} reduce(bf16[256,1,1024]{2,1,0:T(2,128)(2,1)S(1)} %slice_bitcast_fusion.23, bf16[]{:T(256)} %broadcast.215), dimensions={1}, to_apply=%slice_bitcast_fusion.23.reduce_sub_computation | reduce | bytes 1048578
  254.8 4.4 %all-to-all-start.3 = ((bf16[8,2,16384]{2,1,0:T(2,128)(2,1)}), bf16[8,2,16384]{2,1,0:T(2,128)(2,1)}, u32[]{:S(2)}, u32[]{:S(2)}) async-start(bf16[8,2,16384]{2,1,0:T(2,128)(2,1)} %reshape.720), calls=%async_computation.3 | async-start | bytes 1048576 | tf_op jit(solution)/shard_map/all_to_all | solution.py:148
  260.6 3.7 %reduce.30 = bf16[256,1024]{1,0:T(8,128)(2,1)S(1)} reduce(bf16[256,1,1024]{2,1,0:T(2,128)(2,1)S(1)} %slice_bitcast_fusion.22, bf16[]{:T(256)} %broadcast.215), dimensions={1}, to_apply=%slice_bitcast_fusion.22.reduce_sub_computation | reduce | bytes 1048578
  266.3 3.6 %all-to-all-done.3 = bf16[8,2,16384]{2,1,0:T(2,128)(2,1)} async-done(((bf16[8,2,16384]{2,1,0:T(2,128)(2,1)}), bf16[8,2,16384]{2,1,0:T(2,128)(2,1)}, u32[]{:S(2)}, u32[]{:S(2)}) %all-to-all-start.3) | async-done | bytes 524320 | tf_op jit(solution)/shard_map/all_to_all | solution.py:148
  269.9 5.5 %all-to-all-start.2 = ((bf16[8,2,16384]{2,1,0:T(2,128)(2,1)}), bf16[8,2,16384]{2,1,0:T(2,128)(2,1)}, u32[]{:S(2)}, u32[]{:S(2)}) async-start(bf16[8,2,16384]{2,1,0:T(2,128)(2,1)} %reshape.718), calls=%async_computation.2 | async-start | bytes 1048576 | tf_op jit(solution)/shard_map/all_to_all | solution.py:148
  276.1 3.6 %reduce.29 = bf16[256,1024]{1,0:T(8,128)(2,1)S(1)} reduce(bf16[256,1,1024]{2,1,0:T(2,128)(2,1)S(1)} %slice_bitcast_fusion.21, bf16[]{:T(256)} %broadcast.215), dimensions={1}, to_apply=%slice_bitcast_fusion.21.reduce_sub_computation | reduce | bytes 1048578
  280.9 3.6 %reduce.28 = bf16[256,1024]{1,0:T(8,128)(2,1)S(1)} reduce(bf16[256,1,1024]{2,1,0:T(2,128)(2,1)S(1)} %slice_bitcast_fusion.20, bf16[]{:T(256)} %broadcast.215), dimensions={1}, to_apply=%slice_bitcast_fusion.20.reduce_sub_computation | reduce | bytes 1048578
  290.4 6.4 %all-to-all-start.1 = ((bf16[8,2,16384]{2,1,0:T(2,128)(2,1)}), bf16[8,2,16384]{2,1,0:T(2,128)(2,1)S(1)}, u32[]{:S(2)}, u32[]{:S(2)}) async-start(bf16[8,2,16384]{2,1,0:T(2,128)(2,1)} %reshape.716), calls=%async_computation.1 | async-start | bytes 1048576 | tf_op jit(solution)/shard_map/all_to_all | solution.py:148
  300.7 3.1 multiply_reduce_fusion.7
  307.4 7.8 %all-to-all-start = ((bf16[8,2,16384]{2,1,0:T(2,128)(2,1)}), bf16[8,2,16384]{2,1,0:T(2,128)(2,1)}, u32[]{:S(2)}, u32[]{:S(2)}) async-start(bf16[8,2,16384]{2,1,0:T(2,128)(2,1)} %reshape.714), calls=%async_computation | async-start | bytes 1048576 | tf_op jit(solution)/shard_map/all_to_all | solution.py:148
  316.0 2.2 reshape.721
  318.2 2.2 reshape.719
  320.5 1.8 reshape.717
  325.7 3.5 %reshape.715 = bf16[256,1,1024]{2,1,0:T(2,128)(2,1)} reshape(bf16[8,2,16384]{2,1,0:T(2,128)(2,1)} %all-to-all-done) | data formatting | bytes 1048576
  329.1 2.3 bitcast_convert_fusion.3
  331.4 6.1 %multiply_reduce_fusion.3 = (bf16[8,8,4,8,128]{4,3,2,1,0:T(8,128)(2,1)}, bf16[8,8,4,8,128]{4,3,2,1,0:T(8,128)(2,1)}, bf16[8,8,4,8,128]{4,3,2,1,0:T(8,128)(2,1)}, bf16[8,8,4,8,128]{4,3,2,1,0:T(8,128)(2,1)}) fusion(f32[8,8,4,8,128]{4,3,2,1,0:T(8,128)S(1)} %bitcast.303, f32[8,8,8,8]{3,2,1,0:T(8,128)S(1)} %copy.75, f32[8,8,4,8,128]{4,3,2,1,0:T(8,128)S(1)} %bitcast.302, ...), kind=kLoop, calls=%fused_computation.3 | loop fusion | flops 15728640 | bytes 6307840 | tf_op jit(solution)/shard_map/reduce_sum | solution.py:118
  (203 shorter events, 67.4 us)
Async XLA Ops:
  1.6 12.3 %collective-permute-start = (bf16[1,4,6,1024]{3,0,2,1:T(2,128)(2,1)S(1)}, bf16[1,4,6,1024]{3,0,2,1:T(2,128)(2,1)S(1)}, u32[]{:S(2)}, u32[]{:S(2)}) collective-permute-start(bf16[1,4,6,1024]{3,0,2,1:T(2,128)(2,1)S(1)} %copy.168), channel_id=1, source_target_pairs={{0,1},{2,3},{4,5},{6,7},{8,9},{10,11},{12,13},{14,15},{16,17},{18,... | collective-permute-start | bytes 147464 | tf_op jit(solution)/shard_map/ppermute | solution.py:18
  4.1 15.0 %collective-permute-start.1 = (bf16[1,4,6,1024]{3,0,2,1:T(2,128)(2,1)S(1)}, bf16[1,4,6,1024]{3,0,2,1:T(2,128)(2,1)S(1)}, u32[]{:S(2)}, u32[]{:S(2)}) collective-permute-start(bf16[1,4,6,1024]{3,0,2,1:T(2,128)(2,1)S(1)} %copy.169), channel_id=1, source_target_pairs={{1,0},{3,2},{5,4},{7,6},{9,8},{11,10},{13,12},{15,14},{17,16},{19,... | collective-permute-start | bytes 147464 | tf_op jit(solution)/shard_map/ppermute | solution.py:21
  72.6 2.1 copy-start
  76.0 3.5 %copy-start.1 = (bf16[512,256]{1,0:T(8,128)(2,1)S(1)}, bf16[512,256]{1,0:T(8,128)(2,1)}, u32[]{:S(2)}) copy-start(bf16[512,256]{1,0:T(8,128)(2,1)} %constant.50.clone) | copy-start | bytes 786436
  83.2 96.2 %all-to-all-start.11 = ((bf16[8,2,1024]{2,1,0:T(2,128)(2,1)}), bf16[8,2,1024]{2,1,0:T(2,128)(2,1)}, u32[]{:S(2)}, u32[]{:S(2)}) async-start(bf16[8,2,1024]{2,1,0:T(2,128)(2,1)} %reshape.736), calls=%async_computation.11 | async-start | bytes 65536 | tf_op jit(solution)/shard_map/all_to_all | solution.py:148
  100.0 2.8 copy-start.2
  103.5 1.7 copy-start.11
  103.8 1.4 copy-start.8
  153.8 2.8 copy-start.4
  173.4 2.8 copy-start.6
  176.8 0.9 copy-start.25
  177.2 8.2 %copy-start.26 = (bf16[1,64,512]{2,0,1:T(2,128)(2,1)S(1)}, bf16[1,64,512]{2,0,1:T(2,128)(2,1)}, u32[]{:S(2)}) copy-start(bf16[1,64,512]{2,0,1:T(2,128)(2,1)} %get-tuple-element.19) | copy-start | bytes 196612
  177.2 8.2 %copy-start.27 = (f32[64,256]{1,0:T(8,128)S(1)}, f32[64,256]{1,0:T(8,128)}, u32[]{:S(2)}) copy-start(f32[64,256]{1,0:T(8,128)} %fusion.83) | copy-start | bytes 196612
  177.8 27.6 %copy-start.10 = (f32[130,512]{1,0:T(8,128)S(1)}, f32[130,512]{1,0:T(8,128)}, u32[]{:S(2)}) copy-start(f32[130,512]{1,0:T(8,128)} %fusion) | copy-start | bytes 798724
  179.4 12.7 %all-to-all-start.10 = ((bf16[8,2,1024]{2,1,0:T(2,128)(2,1)}), bf16[8,2,1024]{2,1,0:T(2,128)(2,1)S(1)}, u32[]{:S(2)}, u32[]{:S(2)}) async-start(bf16[8,2,1024]{2,1,0:T(2,128)(2,1)} %reshape.734), calls=%async_computation.10 | async-start | bytes 65536 | tf_op jit(solution)/shard_map/all_to_all | solution.py:148
  192.1 10.0 %all-to-all-start.9 = ((bf16[8,2,1024]{2,1,0:T(2,128)(2,1)}), bf16[8,2,1024]{2,1,0:T(2,128)(2,1)S(1)}, u32[]{:S(2)}, u32[]{:S(2)}) async-start(bf16[8,2,1024]{2,1,0:T(2,128)(2,1)} %reshape.732), calls=%async_computation.9 | async-start | bytes 65536 | tf_op jit(solution)/shard_map/all_to_all | solution.py:148
  195.7 19.7 %copy-start.12 = (f32[130,512]{1,0:T(8,128)S(1)}, f32[130,512]{1,0:T(8,128)}, u32[]{:S(2)}) copy-start(f32[130,512]{1,0:T(8,128)} %copy-done.11) | copy-start | bytes 798724
  202.0 10.0 %all-to-all-start.8 = ((bf16[8,2,1024]{2,1,0:T(2,128)(2,1)}), bf16[8,2,1024]{2,1,0:T(2,128)(2,1)S(1)}, u32[]{:S(2)}, u32[]{:S(2)}) async-start(bf16[8,2,1024]{2,1,0:T(2,128)(2,1)} %reshape.730), calls=%async_computation.8 | async-start | bytes 65536 | tf_op jit(solution)/shard_map/all_to_all | solution.py:148
  207.8 18.3 %copy-start.13 = (f32[130,512]{1,0:T(8,128)S(1)}, f32[130,512]{1,0:T(8,128)}, u32[]{:S(2)}) copy-start(f32[130,512]{1,0:T(8,128)} %fusion.2) | copy-start | bytes 798724
  212.0 10.7 %all-to-all-start.7 = ((bf16[8,2,4096]{2,1,0:T(2,128)(2,1)}), bf16[8,2,4096]{2,1,0:T(2,128)(2,1)S(1)}, u32[]{:S(2)}, u32[]{:S(2)}) async-start(bf16[8,2,4096]{2,1,0:T(2,128)(2,1)} %reshape.728), calls=%async_computation.7 | async-start | bytes 262144 | tf_op jit(solution)/shard_map/all_to_all | solution.py:148
  222.7 10.7 %copy-start.17 = (bf16[8,2,4096]{2,1,0:T(2,128)(2,1)}, bf16[8,2,4096]{2,1,0:T(2,128)(2,1)S(1)}, u32[]{:S(2)}) copy-start(bf16[8,2,4096]{2,1,0:T(2,128)(2,1)S(1)} %all-to-all-done.7) | copy-start | bytes 393220
  222.7 10.7 %all-to-all-start.6 = ((bf16[8,2,4096]{2,1,0:T(2,128)(2,1)}), bf16[8,2,4096]{2,1,0:T(2,128)(2,1)S(1)}, u32[]{:S(2)}, u32[]{:S(2)}) async-start(bf16[8,2,4096]{2,1,0:T(2,128)(2,1)} %reshape.726), calls=%async_computation.6 | async-start | bytes 262144 | tf_op jit(solution)/shard_map/all_to_all | solution.py:148
  233.3 10.7 %copy-start.19 = (bf16[8,2,4096]{2,1,0:T(2,128)(2,1)}, bf16[8,2,4096]{2,1,0:T(2,128)(2,1)S(1)}, u32[]{:S(2)}) copy-start(bf16[8,2,4096]{2,1,0:T(2,128)(2,1)S(1)} %all-to-all-done.6) | copy-start | bytes 393220
  233.3 10.7 %all-to-all-start.5 = ((bf16[8,2,4096]{2,1,0:T(2,128)(2,1)}), bf16[8,2,4096]{2,1,0:T(2,128)(2,1)S(1)}, u32[]{:S(2)}, u32[]{:S(2)}) async-start(bf16[8,2,4096]{2,1,0:T(2,128)(2,1)} %reshape.724), calls=%async_computation.5 | async-start | bytes 262144 | tf_op jit(solution)/shard_map/all_to_all | solution.py:148
  244.0 4.3 %copy-start.21 = (bf16[8,2,4096]{2,1,0:T(2,128)(2,1)}, bf16[8,2,4096]{2,1,0:T(2,128)(2,1)S(1)}, u32[]{:S(2)}) copy-start(bf16[8,2,4096]{2,1,0:T(2,128)(2,1)S(1)} %all-to-all-done.5) | copy-start | bytes 393220
  244.0 10.8 %all-to-all-start.4 = ((bf16[8,2,4096]{2,1,0:T(2,128)(2,1)}), bf16[8,2,4096]{2,1,0:T(2,128)(2,1)S(1)}, u32[]{:S(2)}, u32[]{:S(2)}) async-start(bf16[8,2,4096]{2,1,0:T(2,128)(2,1)} %reshape.722), calls=%async_computation.4 | async-start | bytes 262144 | tf_op jit(solution)/shard_map/all_to_all | solution.py:148
  251.9 7.3 %copy-start.28 = (s32[8,8,8]{2,1,0:T(8,128)S(1)}, s32[8,8,8]{2,1,0:T(8,128)}, u32[]{:S(2)}) copy-start(s32[8,8,8]{2,1,0:T(8,128)} %param.16) | copy-start | bytes 6148
  251.9 7.3 %copy-start.29 = (f32[8,8,8]{2,0,1:T(8,128)S(1)}, f32[8,8,8]{2,0,1:T(8,128)}, u32[]{:S(2)}) copy-start(f32[8,8,8]{2,0,1:T(8,128)} %multiply_add_fusion.4) | copy-start | bytes 6148
  252.0 7.4 %copy-start.30 = (f32[8,8,8]{2,0,1:T(8,128)S(1)}, f32[8,8,8]{2,0,1:T(8,128)}, u32[]{:S(2)}) copy-start(f32[8,8,8]{2,0,1:T(8,128)} %convolution_divide_fusion) | copy-start | bytes 6148
  252.0 7.4 %copy-start.31 = (f32[8,8,1,1]{1,0,3,2:T(8,128)S(1)}, f32[8,8,1,1]{1,0,3,2:T(8,128)}, u32[]{:S(2)}) copy-start(f32[8,8,1,1]{1,0,3,2:T(8,128)} %constant.62) | copy-start | bytes 772
  252.0 7.4 %copy-start.32 = (f32[8,8]{0,1:T(8,128)S(1)}, f32[8,8]{0,1:T(8,128)}, u32[]{:S(2)}) copy-start(f32[8,8]{0,1:T(8,128)} %constant.63) | copy-start | bytes 772
  253.2 6.7 %copy-start.3 = (f32[1,262,1024]{2,0,1:T(1,128)S(1)}, f32[1,262,1024]{2,0,1:T(1,128)}, u32[]{:S(2)}) copy-start(f32[1,262,1024]{2,0,1:T(1,128)} %copy-done.2) | copy-start | bytes 3219460
  254.8 5.0 %copy-start.23 = (bf16[8,2,4096]{2,1,0:T(2,128)(2,1)}, bf16[8,2,4096]{2,1,0:T(2,128)(2,1)S(1)}, u32[]{:S(2)}) copy-start(bf16[8,2,4096]{2,1,0:T(2,128)(2,1)S(1)} %all-to-all-done.4) | copy-start | bytes 393220
  254.8 15.0 %all-to-all-start.3 = ((bf16[8,2,16384]{2,1,0:T(2,128)(2,1)}), bf16[8,2,16384]{2,1,0:T(2,128)(2,1)}, u32[]{:S(2)}, u32[]{:S(2)}) async-start(bf16[8,2,16384]{2,1,0:T(2,128)(2,1)} %reshape.720), calls=%async_computation.3 | async-start | bytes 1048576 | tf_op jit(solution)/shard_map/all_to_all | solution.py:148
  260.6 4.9 %copy-start.5 = (f32[1,262,1024]{2,0,1:T(1,128)S(1)}, f32[1,262,1024]{2,0,1:T(1,128)}, u32[]{:S(2)}) copy-start(f32[1,262,1024]{2,0,1:T(1,128)} %copy-done.4) | copy-start | bytes 3219460
  265.5 9.8 %copy-start.7 = (f32[1,262,1024]{2,0,1:T(1,128)S(1)}, f32[1,262,1024]{2,0,1:T(1,128)}, u32[]{:S(2)}) copy-start(f32[1,262,1024]{2,0,1:T(1,128)} %copy-done.6) | copy-start | bytes 3219460
  269.9 20.5 %all-to-all-start.2 = ((bf16[8,2,16384]{2,1,0:T(2,128)(2,1)}), bf16[8,2,16384]{2,1,0:T(2,128)(2,1)}, u32[]{:S(2)}, u32[]{:S(2)}) async-start(bf16[8,2,16384]{2,1,0:T(2,128)(2,1)} %reshape.718), calls=%async_computation.2 | async-start | bytes 1048576 | tf_op jit(solution)/shard_map/all_to_all | solution.py:148
  287.8 2.5 copy-start.18
  290.4 7.3 %copy-start.20 = (bf16[8,2,4096]{2,1,0:T(2,128)(2,1)S(1)}, bf16[8,2,4096]{2,1,0:T(2,128)(2,1)}, u32[]{:S(2)}) copy-start(bf16[8,2,4096]{2,1,0:T(2,128)(2,1)} %copy-done.19) | copy-start | bytes 393220
  290.4 17.0 %all-to-all-start.1 = ((bf16[8,2,16384]{2,1,0:T(2,128)(2,1)}), bf16[8,2,16384]{2,1,0:T(2,128)(2,1)S(1)}, u32[]{:S(2)}, u32[]{:S(2)}) async-start(bf16[8,2,16384]{2,1,0:T(2,128)(2,1)} %reshape.716), calls=%async_computation.1 | async-start | bytes 1048576 | tf_op jit(solution)/shard_map/all_to_all | solution.py:148
  297.5 1.2 copy-start.22
  298.6 1.2 copy-start.24
  307.4 18.3 %all-to-all-start = ((bf16[8,2,16384]{2,1,0:T(2,128)(2,1)}), bf16[8,2,16384]{2,1,0:T(2,128)(2,1)}, u32[]{:S(2)}, u32[]{:S(2)}) async-start(bf16[8,2,16384]{2,1,0:T(2,128)(2,1)} %reshape.714), calls=%async_computation | async-start | bytes 1048576 | tf_op jit(solution)/shard_map/all_to_all | solution.py:148
  323.3 1.2 copy-start.9
  337.5 1.4 copy-start.16
  337.5 1.6 copy-start.15
  338.9 1.0 copy-start.14
where the time goes:
time: 348 us; the launch traced here: 342 us
  other arithmetic  180 us (52%)
  starting transfers between devices  61.1 us (18%)
  local copies, waits for them, and re-layouts  55.6 us (16%)
  waiting for transfers between devices  35.1 us (10%)
  matrix products  7.96 us (2%)
    add x2, other arithmetic, column_taps(): total = total + taps[k] * wide[..., k:k + width]  76 us
    all_to_all x12, starting transfers between devices, local(): lax.all_to_all(level, 'date', split_axis=1, concat_axis=0, tiled=True)  57.4 us
    select_n x8, other arithmetic, keep_rows(): return jnp.where(inside[None, :, None], values, 0.0)  39.8 us
    all_to_all x12, waiting for transfers between devices, local(): lax.all_to_all(level, 'date', split_axis=1, concat_axis=0, tiled=True)  35.1 us
    unnamed x99, local copies, waits for them, and re-layouts  31.5 us
    unnamed x12, other arithmetic  23.6 us
    convert_element_type x8, other arithmetic, halve_columns(): low = (values - high.astype(jnp.float32)).astype(jnp.bfloat16)  10.9 us
    reduce_sum x3, other arithmetic, smooth(): return jnp.sum(grown * values[None], axis=1).astype(jnp.bfloat16)  10.4 us
  transfers between devices with their start and end apart: 14, of which 9 were waited for; matrix products, arithmetic and copies ran while one was open for 48% of the time, Pallas kernels for 0%

commit v1 on v0

--- a/solution.py
+++ b/solution.py
@@ -144,10 +144,32 @@
         level_zero = resampled_wide[:, 3 : 3 + rows].astype(jnp.bfloat16)
         level_one = half_wide[:, 1 : 1 + rows // 2].astype(jnp.bfloat16)
         level_two = decimate_rim(half_wide).astype(jnp.bfloat16)
-        got = [
-            lax.all_to_all(level, "date", split_axis=1, concat_axis=0, tiled=True)
-            for level in (level_zero, level_one, level_two)
-        ]
+
+        def space_wrap(incoming_x):
+            axis_key = "date"
+            built, response = (lax.psum(1, axis_key), lax.axis_index(axis_key))
+            arr_now = incoming_x.shape[1] // built
+            tile_out = list(incoming_x.shape)
+            tile_out[1] = arr_now
+            item_now = tile_out[0]
+            tile_out[0] = item_now * built
+            o_now = jnp.zeros(tile_out, incoming_x.dtype)
+            nth = 0
+            while nth < built:
+                reached = lax.dynamic_slice_in_dim(
+                    incoming_x, (response ^ nth) * arr_now, arr_now, axis=1
+                )
+                if nth:
+                    reached = lax.ppermute(
+                        reached, axis_key, [(pp, pp ^ nth) for pp in range(built)]
+                    )
+                o_now = lax.dynamic_update_slice_in_dim(
+                    o_now, reached, (response ^ nth) * item_now, axis=0
+                )
+                nth += 1
+            return o_now
+
+        got = [space_wrap(level) for level in (level_zero, level_one, level_two)]
         fine.append(smooth(got[0], coeff, fine_rows // mask_rows, width // mask_cols))
         half.append(smooth(got[1], coeff, fine_rows // 2 // mask_rows, width // 2 // mask_cols))
         quarter.append(smooth(got[2], coeff, fine_rows // 4 // mask_rows, width // 4 // mask_cols))

time: 348 us -> 336 us (0.966)
  other arithmetic: 180 us -> 89.7 us
  starting transfers between devices: 61.1 us -> 139 us
  local copies, waits for them, and re-layouts: 55.6 us -> 72.8 us
  waiting for transfers between devices: 35.1 us -> 19.7 us
    ppermute x0 -> x84, starting transfers between devices: none -> 135 us  [space_wrap(): lax.ppermute(reached, axis_key, [(pp, pp ^ nth) for pp in range(built)])]
    all_to_all x12 -> x0, starting transfers between devices: 57.4 us -> none  [local(): lax.all_to_all(level, 'date', split_axis=1, concat_axis=0, tiled=True)]
    add x2, other arithmetic: 76 us -> 31.7 us  [column_taps(): total = total + taps[k] * wide[..., k:k + width]]
    all_to_all x12 -> x0, waiting for transfers between devices: 35.1 us -> none  [local(): lax.all_to_all(level, 'date', split_axis=1, concat_axis=0, tiled=True)]
    unnamed x99 -> x102, local copies, waits for them, and re-layouts: 31.5 us -> 0.66 us
    unnamed x12 -> x0, other arithmetic: 23.6 us -> none
    ppermute x0 -> x84, waiting for transfers between devices: none -> 19.7 us  [space_wrap(): lax.ppermute(reached, axis_key, [(pp, pp ^ nth) for pp in range(built)])]
    dynamic_update_slice x0 -> x88, local copies, waits for them, and re-layouts: none -> 16.4 us  [space_wrap(): lax.dynamic_update_slice_in_dim(o_now, reached, (response ^ nth) * item_n...]
  transfers between devices with their start and end apart: 14 -> 86, of which waited for: 9 -> 8; matrix products, arithmetic and copies ran while one was open for 48% -> 18% of each run, Pallas kernels for 0% -> 0%
where the time goes in v1:
time: 336 us; the launch traced here: 331 us
  starting transfers between devices  139 us (41%)
  other arithmetic  89.7 us (27%)
  local copies, waits for them, and re-layouts  72.8 us (22%)
  waiting for transfers between devices  19.7 us (6%)
  matrix products  7.45 us (2%)
    ppermute x84, starting transfers between devices, space_wrap(): lax.ppermute(reached, axis_key, [(pp, pp ^ nth) for pp in range(built)])  135 us
    add x2, other arithmetic, column_taps(): total = total + taps[k] * wide[..., k:k + width]  31.7 us
    select_n x8, other arithmetic, keep_rows(): return jnp.where(inside[None, :, None], values, 0.0)  28 us
    ppermute x84, waiting for transfers between devices, space_wrap(): lax.ppermute(reached, axis_key, [(pp, pp ^ nth) for pp in range(built)])  19.7 us
    dynamic_update_slice x88, local copies, waits for them, and re-layouts, space_wrap(): lax.dynamic_update_slice_in_dim(o_now, reached, (response ^ nth) * item_n...  16.4 us
    reshape x8, local copies, waits for them, and re-layouts, halve_rows(): extended.reshape(extended.shape[:1] + (pairs_count, 2) + extended.shape[2:])  16 us
    reduce_sum x3, other arithmetic, smooth(): return jnp.sum(grown * values[None], axis=1).astype(jnp.bfloat16)  11.5 us
    convert_element_type x8, other arithmetic, halve_columns(): low = (values - high.astype(jnp.float32)).astype(jnp.bfloat16)  9.8 us
  transfers between devices with their start and end apart: 86, of which 8 were waited for; matrix products, arithmetic and copies ran while one was open for 18% of the time, Pallas kernels for 0%

profile of v1, /device:TPU:0, one launch (start us, length us, event | category | flops | bytes accessed | tf_op | source)
XLA Modules:
  0.0 331.3 jit_solution(13600172435750628874)
XLA Ops:
  1.5 2.4 collective-permute-start
  14.9 2.2 pad_maximum_fusion
  18.9 12.8 %fusion.38 = (f32[1,268,1024]{2,1,0:T(8,128)S(1)}, f32[1,268,1024]{2,1,0:T(8,128)S(1)}) fusion(f32[1,268,1024]{2,1,0:T(8,128)S(1)} %get-tuple-element.32, f32[]{:T(128)} %bitcast.46, f32[]{:T(128)} %bitcast.45, f32[]{:T(128)} %bitcast.44, f32[]{:T(128)} %bitcast.42, f32[]{:T(128)} %bitcast.41, f32[]{:T(128)} %bitcast.40, f32[]{:T(128)} %bitcast.38, ...), kind=kLoop, calls=%fused_computation.84 | loop fusion | flops 7135232 | bytes 4390968 | tf_op jit(solution)/shard_map/add | solution.py:31
  31.7 5.4 %fusion.57 = f32[1,262,1024]{2,1,0:T(8,128)S(1)} fusion(f32[1,268,1024]{2,1,0:T(8,128)S(1)} %get-tuple-element.204, f32[]{:T(128)} %bitcast.69, f32[]{:T(128)} %bitcast.68, f32[]{:T(128)} %bitcast.67, f32[]{:T(128)} %bitcast.66, f32[]{:T(128)} %bitcast.65, f32[]{:T(128)} %bitcast.64, f32[]{:T(128)} %bitcast.54, pred[262]{0:T(512)(128)(4,1)S(1)} %fusion.165), kind=kLoop, calls=%fused_computation.105 | loop fusion | flops 3756032 | bytes 8585506 | tf_op jit(solution)/shard_map/jit(_where)/select_n | solution.py:83
  37.0 2.3 reshape.630
  48.3 6.3 %fusion.64 = f32[1,262,1024]{2,1,0:T(8,128)} fusion(f32[1,268,1024]{2,1,0:T(8,128)S(1)} %get-tuple-element.203, f32[]{:T(128)} %bitcast.52, f32[]{:T(128)} %bitcast.51, f32[]{:T(128)} %bitcast.50, f32[]{:T(128)} %bitcast.49, f32[]{:T(128)} %bitcast.48, f32[]{:T(128)} %bitcast.47, f32[]{:T(128)} %bitcast.37, pred[262]{0:T(512)(128)(4,1)S(1)} %fusion.165), kind=kLoop, calls=%fused_computation.119 | loop fusion | flops 3756032 | bytes 8585506 | tf_op jit(solution)/shard_map/jit(_where)/select_n | solution.py:83
  54.6 2.6 reshape.627
  62.3 18.9 %fusion.14 = (f32[1,268,1024]{2,1,0:T(8,128)S(1)}, f32[1,268,1024]{2,1,0:T(8,128)S(1)}) fusion(f32[1,268,1024]{2,1,0:T(8,128)} %get-tuple-element.34, f32[]{:T(128)} %bitcast.12, f32[]{:T(128)} %bitcast.11, f32[]{:T(128)} %bitcast.10, f32[]{:T(128)} %bitcast.8, f32[]{:T(128)} %bitcast.7, f32[]{:T(128)} %bitcast.6, f32[]{:T(128)} %bitcast.4, f32[]{:T(128)} %bitcast.29, ...), kind=kLoop, calls=%fused_computation.60 | loop fusion | flops 7135232 | bytes 4390968 | tf_op jit(solution)/shard_map/add | solution.py:31
  81.2 6.2 %fusion.71 = f32[1,262,1024]{2,1,0:T(8,128)} fusion(f32[1,268,1024]{2,1,0:T(8,128)S(1)} %get-tuple-element.202, f32[]{:T(128)} %bitcast.35, f32[]{:T(128)} %bitcast.34, f32[]{:T(128)} %bitcast.33, f32[]{:T(128)} %bitcast.32, f32[]{:T(128)} %bitcast.31, f32[]{:T(128)} %bitcast.30, f32[]{:T(128)} %bitcast.20, pred[262]{0:T(512)(128)(4,1)S(1)} %fusion.165), kind=kLoop, calls=%fused_computation.133 | loop fusion | flops 3756032 | bytes 8585506 | tf_op jit(solution)/shard_map/jit(_where)/select_n | solution.py:83
  87.4 3.5 %reshape.624 = f32[1,131,2,1024]{3,0,2,1:T(1,128)} reshape(f32[1,262,1024]{2,1,0:T(8,128)} %fusion.71) | data formatting | bytes 2146304 | tf_op jit(solution)/shard_map/reshape | solution.py:65
  99.8 6.2 %fusion.78 = f32[1,262,1024]{2,1,0:T(8,128)} fusion(f32[1,268,1024]{2,1,0:T(8,128)S(1)} %get-tuple-element.201, f32[]{:T(128)} %bitcast.18, f32[]{:T(128)} %bitcast.17, f32[]{:T(128)} %bitcast.16, f32[]{:T(128)} %bitcast.15, f32[]{:T(128)} %bitcast.14, f32[]{:T(128)} %bitcast.13, f32[]{:T(128)} %bitcast.3, pred[262]{0:T(512)(128)(4,1)S(1)} %fusion.165), kind=kLoop, calls=%fused_computation.147 | loop fusion | flops 3756032 | bytes 8585506 | tf_op jit(solution)/shard_map/jit(_where)/select_n | solution.py:83
  106.0 2.6 reshape.621
  109.4 2.3 subtract_convert_fusion.3
  117.7 2.4 collective-permute-start.79
  121.7 3.0 collective-permute-start.82
  136.9 3.4 %collective-permute-done.72 = bf16[1,8,256]{2,1,0:T(8,128)(2,1)S(1)} collective-permute-done((bf16[1,8,256]{2,1,0:T(8,128)(2,1)S(1)}, bf16[1,8,256]{2,1,0:T(8,128)(2,1)S(1)}, u32[]{:S(2)}, u32[]{:S(2)}) %collective-permute-start.72) | collective-permute-done | bytes 4128 | tf_op jit(solution)/shard_map/ppermute | solution.py:163
  140.3 3.6 %collective-permute-start.84 = (bf16[1,8,256]{2,1,0:T(8,128)(2,1)S(1)}, bf16[1,8,256]{2,1,0:T(8,128)(2,1)S(1)}, u32[]{:S(2)}, u32[]{:S(2)}) collective-permute-start(bf16[1,8,256]{2,1,0:T(8,128)(2,1)S(1)} %get-tuple-element.118), channel_id=1, source_target_pairs={{0,12},{2,14},{4,8},{6,10},{8,4},{10,6},{12,0},{14,2},{1,13},{3,15... | collective-permute-start | bytes 12296 | tf_op jit(solution)/shard_map/ppermute | solution.py:163
  144.0 3.6 %collective-permute-done.73 = bf16[1,8,256]{2,1,0:T(8,128)(2,1)S(1)} collective-permute-done((bf16[1,8,256]{2,1,0:T(8,128)(2,1)S(1)}, bf16[1,8,256]{2,1,0:T(8,128)(2,1)S(1)}, u32[]{:S(2)}, u32[]{:S(2)}) %collective-permute-start.73) | collective-permute-done | bytes 4128 | tf_op jit(solution)/shard_map/ppermute | solution.py:163
  148.4 3.7 %collective-permute-done.74 = bf16[1,8,256]{2,1,0:T(8,128)(2,1)S(1)} collective-permute-done((bf16[1,8,256]{2,1,0:T(8,128)(2,1)S(1)}, bf16[1,8,256]{2,1,0:T(8,128)(2,1)S(1)}, u32[]{:S(2)}, u32[]{:S(2)}) %collective-permute-start.74) | collective-permute-done | bytes 4128 | tf_op jit(solution)/shard_map/ppermute | solution.py:163
  152.1 2.3 collective-permute-start.75
  156.6 3.7 %collective-permute-start.77 = (bf16[1,8,256]{2,1,0:T(8,128)(2,1)S(1)}, bf16[1,8,256]{2,1,0:T(8,128)(2,1)S(1)}, u32[]{:S(2)}, u32[]{:S(2)}) collective-permute-start(bf16[1,8,256]{2,1,0:T(8,128)(2,1)S(1)} %get-tuple-element.125), channel_id=1, source_target_pairs={{0,12},{2,14},{4,8},{6,10},{8,4},{10,6},{12,0},{14,2},{1,13},{3,15... | collective-permute-start | bytes 12296 | tf_op jit(solution)/shard_map/ppermute | solution.py:163
  167.8 3.7 %collective-permute-start.70 = (bf16[1,8,256]{2,1,0:T(8,128)(2,1)S(1)}, bf16[1,8,256]{2,1,0:T(8,128)(2,1)S(1)}, u32[]{:S(2)}, u32[]{:S(2)}) collective-permute-start(bf16[1,8,256]{2,1,0:T(8,128)(2,1)S(1)} %get-tuple-element.132), channel_id=1, source_target_pairs={{0,12},{2,14},{4,8},{6,10},{8,4},{10,6},{12,0},{14,2},{1,13},{3,15... | collective-permute-start | bytes 12296 | tf_op jit(solution)/shard_map/ppermute | solution.py:163
  173.2 3.0 collective-permute-start.60
  179.0 3.7 %collective-permute-start.63 = (bf16[1,8,256]{2,1,0:T(8,128)(2,1)S(1)}, bf16[1,8,256]{2,1,0:T(8,128)(2,1)S(1)}, u32[]{:S(2)}, u32[]{:S(2)}) collective-permute-start(bf16[1,8,256]{2,1,0:T(8,128)(2,1)S(1)} %get-tuple-element.139), channel_id=1, source_target_pairs={{0,12},{2,14},{4,8},{6,10},{8,4},{10,6},{12,0},{14,2},{1,13},{3,15... | collective-permute-start | bytes 12296 | tf_op jit(solution)/shard_map/ppermute | solution.py:163
  184.4 3.0 collective-permute-start.53
  190.8 2.3 multiply_reduce_fusion.11
  198.1 3.7 %collective-permute-start.56 = (bf16[1,16,512]{2,1,0:T(8,128)(2,1)}, bf16[1,16,512]{2,1,0:T(8,128)(2,1)S(1)}, u32[]{:S(2)}, u32[]{:S(2)}) collective-permute-start(bf16[1,16,512]{2,1,0:T(8,128)(2,1)} %get-tuple-element.86), channel_id=1, source_target_pairs={{0,12},{2,14},{4,8},{6,10},{8,4},{10,6},{12,0},{14,2},{1,13},{3,15... | collective-permute-start | bytes 49160 | tf_op jit(solution)/shard_map/ppermute | solution.py:163
  208.7 3.1 collective-permute-start.46
  217.0 3.7 %collective-permute-start.49 = (bf16[1,16,512]{2,1,0:T(8,128)(2,1)S(1)}, bf16[1,16,512]{2,1,0:T(8,128)(2,1)S(1)}, u32[]{:S(2)}, u32[]{:S(2)}) collective-permute-start(bf16[1,16,512]{2,1,0:T(8,128)(2,1)S(1)} %copy-done.47), channel_id=1, source_target_pairs={{0,12},{2,14},{4,8},{6,10},{8,4},{10,6},{12,0},{14,2},{1,13},{3,15... | collective-permute-start | bytes 49160 | tf_op jit(solution)/shard_map/ppermute | solution.py:163
  222.6 3.1 collective-permute-start.39
  225.7 2.3 collective-permute-start.40
  228.7 3.7 %collective-permute-start.42 = (bf16[1,16,512]{2,1,0:T(8,128)(2,1)S(1)}, bf16[1,16,512]{2,1,0:T(8,128)(2,1)S(1)}, u32[]{:S(2)}, u32[]{:S(2)}) collective-permute-start(bf16[1,16,512]{2,1,0:T(8,128)(2,1)S(1)} %copy-done.40), channel_id=1, source_target_pairs={{0,12},{2,14},{4,8},{6,10},{8,4},{10,6},{12,0},{14,2},{1,13},{3,15... | collective-permute-start | bytes 49160 | tf_op jit(solution)/shard_map/ppermute | solution.py:163
  234.3 3.1 collective-permute-start.32
  237.4 2.3 collective-permute-start.33
  240.4 3.7 %collective-permute-start.35 = (bf16[1,16,512]{2,1,0:T(8,128)(2,1)S(1)}, bf16[1,16,512]{2,1,0:T(8,128)(2,1)S(1)}, u32[]{:S(2)}, u32[]{:S(2)}) collective-permute-start(bf16[1,16,512]{2,1,0:T(8,128)(2,1)S(1)} %copy-done.33), channel_id=1, source_target_pairs={{0,12},{2,14},{4,8},{6,10},{8,4},{10,6},{12,0},{14,2},{1,13},{3,15... | collective-permute-start | bytes 49160 | tf_op jit(solution)/shard_map/ppermute | solution.py:163
  248.1 3.1 collective-permute-start.25
  262.4 4.3 %multiply_reduce_fusion.7 = (bf16[8,8,2,8,64]{4,3,2,1,0:T(8,128)(2,1)}, bf16[8,8,2,8,64]{4,3,2,1,0:T(8,128)(2,1)}, bf16[8,8,2,8,64]{4,3,2,1,0:T(8,128)(2,1)}, bf16[8,8,2,8,64]{4,3,2,1,0:T(8,128)(2,1)}) fusion(f32[8,8,2,8,64]{4,3,2,1,0:T(8,128)} %reshape.653, f32[8,8,8,8]{3,2,1,0:T(8,128)S(1)} %copy.50, f32[8,8,2,8,64]{4,3,2,1,0:T(8,128)} %reshape.654, ...), kind=kLoop, calls=%fused_computation.7 | loop fusion | flops 3932160 | bytes 1589248 | tf_op jit(solution)/shard_map/reduce_sum | solution.py:118
  271.3 3.7 %collective-permute-start.28 = (bf16[1,32,1024]{2,1,0:T(8,128)(2,1)}, bf16[1,32,1024]{2,1,0:T(8,128)(2,1)S(1)}, u32[]{:S(2)}, u32[]{:S(2)}) collective-permute-start(bf16[1,32,1024]{2,1,0:T(8,128)(2,1)} %get-tuple-element.46), channel_id=1, source_target_pairs={{0,12},{2,14},{4,8},{6,10},{8,4},{10,6},{12,0},{14,2},{1,13},{3,15... | collective-permute-start | bytes 196616 | tf_op jit(solution)/shard_map/ppermute | solution.py:163
  279.4 3.1 collective-permute-start.18
  283.4 2.3 collective-permute-start.19
  286.5 3.8 %collective-permute-start.21 = (bf16[1,32,1024]{2,1,0:T(8,128)(2,1)S(1)}, bf16[1,32,1024]{2,1,0:T(8,128)(2,1)S(1)}, u32[]{:S(2)}, u32[]{:S(2)}) collective-permute-start(bf16[1,32,1024]{2,1,0:T(8,128)(2,1)S(1)} %copy-done.31), channel_id=1, source_target_pairs={{0,12},{2,14},{4,8},{6,10},{8,4},{10,6},{12,0},{14,2},{1,13},{3,15... | collective-permute-start | bytes 196616 | tf_op jit(solution)/shard_map/ppermute | solution.py:163
  293.1 2.9 collective-permute-done.20
  296.1 4.9 %collective-permute-start.12 = (bf16[1,32,1024]{2,1,0:T(8,128)(2,1)S(1)}, bf16[1,32,1024]{2,1,0:T(8,128)(2,1)S(1)}, u32[]{:S(2)}, u32[]{:S(2)}) collective-permute-start(bf16[1,32,1024]{2,1,0:T(8,128)(2,1)S(1)} %copy-done.26), channel_id=1, source_target_pairs={{0,8},{2,10},{4,12},{6,14},{8,0},{10,2},{12,4},{14,6},{1,9},{3,11}... | collective-permute-start | bytes 196616 | tf_op jit(solution)/shard_map/ppermute | solution.py:163
  302.1 2.3 collective-permute-start.14
  311.5 2.4 collective-permute-start.6
  314.0 2.3 collective-permute-start.7
  320.3 3.1 collective-permute-done.8
  323.6 5.0 %multiply_reduce_fusion.3 = (bf16[8,8,4,8,128]{4,3,2,1,0:T(8,128)(2,1)S(1)}, bf16[8,8,4,8,128]{4,3,2,1,0:T(8,128)(2,1)S(1)}, bf16[8,8,4,8,128]{4,3,2,1,0:T(8,128)(2,1)S(1)}, bf16[8,8,4,8,128]{4,3,2,1,0:T(8,128)(2,1)S(1)}) fusion(f32[8,8,4,8,128]{4,3,2,1,0:T(8,128)S(1)} %bitcast.319, f32[8,8,8,8]{3,2,1,0:T(8,128)S(1)} %copy.50, ...), kind=kLoop, calls=%fused_computation.3 | loop fusion | flops 15728640 | bytes 6307840 | tf_op jit(solution)/shard_map/reduce_sum | solution.py:118
  (438 shorter events, 141.8 us)
Async XLA Ops:
  1.5 13.3 %collective-permute-start = (bf16[1,4,6,1024]{3,2,1,0:T(8,128)(2,1)S(1)}, bf16[1,4,6,1024]{3,2,1,0:T(8,128)(2,1)S(1)}, u32[]{:S(2)}, u32[]{:S(2)}) collective-permute-start(bf16[1,4,6,1024]{3,2,1,0:T(8,128)(2,1)S(1)} %get-tuple-element.35), channel_id=1, source_target_pairs={{0,1},{2,3},{4,5},{6,7},{8,9},{10,11},{12,13},{14,15},{16,17},{18,... | collective-permute-start | bytes 147464 | tf_op jit(solution)/shard_map/ppermute | solution.py:18
  3.9 11.0 %collective-permute-start.1 = (bf16[1,4,6,1024]{3,2,1,0:T(8,128)(2,1)S(1)}, bf16[1,4,6,1024]{3,2,1,0:T(8,128)(2,1)S(1)}, u32[]{:S(2)}, u32[]{:S(2)}) collective-permute-start(bf16[1,4,6,1024]{3,2,1,0:T(8,128)(2,1)S(1)} %get-tuple-element.36), channel_id=1, source_target_pairs={{1,0},{3,2},{5,4},{7,6},{9,8},{11,10},{13,12},{15,14},{17,16},{19,... | collective-permute-start | bytes 147464 | tf_op jit(solution)/shard_map/ppermute | solution.py:21
  117.7 18.9 %collective-permute-start.79 = (bf16[1,8,256]{2,1,0:T(8,128)(2,1)S(1)}, bf16[1,8,256]{2,1,0:T(8,128)(2,1)S(1)}, u32[]{:S(2)}, u32[]{:S(2)}) collective-permute-start(bf16[1,8,256]{2,1,0:T(8,128)(2,1)S(1)} %get-tuple-element.123), channel_id=1, source_target_pairs={{0,2},{2,0},{4,6},{6,4},{8,10},{10,8},{12,14},{14,12},{1,3},{3,1},... | collective-permute-start | bytes 12296 | tf_op jit(solution)/shard_map/ppermute | solution.py:163
  120.1 23.8 %collective-permute-start.80 = (bf16[1,8,256]{2,1,0:T(8,128)(2,1)S(1)}, bf16[1,8,256]{2,1,0:T(8,128)(2,1)S(1)}, u32[]{:S(2)}, u32[]{:S(2)}) collective-permute-start(bf16[1,8,256]{2,1,0:T(8,128)(2,1)S(1)} %get-tuple-element.122), channel_id=1, source_target_pairs={{0,4},{2,6},{4,0},{6,2},{8,12},{10,14},{12,8},{14,10},{1,5},{3,7},... | collective-permute-start | bytes 12296 | tf_op jit(solution)/shard_map/ppermute | solution.py:163
  121.7 25.9 %collective-permute-start.81 = (bf16[1,8,256]{2,1,0:T(8,128)(2,1)S(1)}, bf16[1,8,256]{2,1,0:T(8,128)(2,1)S(1)}, u32[]{:S(2)}, u32[]{:S(2)}) collective-permute-start(bf16[1,8,256]{2,1,0:T(8,128)(2,1)S(1)} %get-tuple-element.121), channel_id=1, source_target_pairs={{0,6},{2,4},{4,2},{6,0},{8,14},{10,12},{12,10},{14,8},{1,7},{3,5},... | collective-permute-start | bytes 12296 | tf_op jit(solution)/shard_map/ppermute | solution.py:163
  121.7 32.8 %collective-permute-start.82 = (bf16[1,8,256]{2,1,0:T(8,128)(2,1)S(1)}, bf16[1,8,256]{2,1,0:T(8,128)(2,1)S(1)}, u32[]{:S(2)}, u32[]{:S(2)}) collective-permute-start(bf16[1,8,256]{2,1,0:T(8,128)(2,1)S(1)} %get-tuple-element.120), channel_id=1, source_target_pairs={{0,8},{2,10},{4,12},{6,14},{8,0},{10,2},{12,4},{14,6},{1,9},{3,11}... | collective-permute-start | bytes 12296 | tf_op jit(solution)/shard_map/ppermute | solution.py:163
  124.7 35.7 %collective-permute-start.83 = (bf16[1,8,256]{2,1,0:T(8,128)(2,1)S(1)}, bf16[1,8,256]{2,1,0:T(8,128)(2,1)S(1)}, u32[]{:S(2)}, u32[]{:S(2)}) collective-permute-start(bf16[1,8,256]{2,1,0:T(8,128)(2,1)S(1)} %get-tuple-element.119), channel_id=1, source_target_pairs={{0,10},{2,8},{4,14},{6,12},{8,2},{10,0},{12,6},{14,4},{1,11},{3,9}... | collective-permute-start | bytes 12296 | tf_op jit(solution)/shard_map/ppermute | solution.py:163
  140.3 21.6 %collective-permute-start.84 = (bf16[1,8,256]{2,1,0:T(8,128)(2,1)S(1)}, bf16[1,8,256]{2,1,0:T(8,128)(2,1)S(1)}, u32[]{:S(2)}, u32[]{:S(2)}) collective-permute-start(bf16[1,8,256]{2,1,0:T(8,128)(2,1)S(1)} %get-tuple-element.118), channel_id=1, source_target_pairs={{0,12},{2,14},{4,8},{6,10},{8,4},{10,6},{12,0},{14,2},{1,13},{3,15... | collective-permute-start | bytes 12296 | tf_op jit(solution)/shard_map/ppermute | solution.py:163
  147.5 17.5 %collective-permute-start.85 = (bf16[1,8,256]{2,1,0:T(8,128)(2,1)S(1)}, bf16[1,8,256]{2,1,0:T(8,128)(2,1)S(1)}, u32[]{:S(2)}, u32[]{:S(2)}) collective-permute-start(bf16[1,8,256]{2,1,0:T(8,128)(2,1)S(1)} %get-tuple-element.117), channel_id=1, source_target_pairs={{0,14},{2,12},{4,10},{6,8},{8,6},{10,4},{12,2},{14,0},{1,15},{3,13... | collective-permute-start | bytes 12296 | tf_op jit(solution)/shard_map/ppermute | solution.py:163
  162.0 9.6 %collective-permute-start.66 = (bf16[1,8,256]{2,1,0:T(8,128)(2,1)S(1)}, bf16[1,8,256]{2,1,0:T(8,128)(2,1)S(1)}, u32[]{:S(2)}, u32[]{:S(2)}) collective-permute-start(bf16[1,8,256]{2,1,0:T(8,128)(2,1)S(1)} %get-tuple-element.136), channel_id=1, source_target_pairs={{0,4},{2,6},{4,0},{6,2},{8,12},{10,14},{12,8},{14,10},{1,5},{3,7},... | collective-permute-start | bytes 12296 | tf_op jit(solution)/shard_map/ppermute | solution.py:163
  163.3 9.4 %collective-permute-start.67 = (bf16[1,8,256]{2,1,0:T(8,128)(2,1)S(1)}, bf16[1,8,256]{2,1,0:T(8,128)(2,1)S(1)}, u32[]{:S(2)}, u32[]{:S(2)}) collective-permute-start(bf16[1,8,256]{2,1,0:T(8,128)(2,1)S(1)} %get-tuple-element.135), channel_id=1, source_target_pairs={{0,6},{2,4},{4,2},{6,0},{8,14},{10,12},{12,10},{14,8},{1,7},{3,5},... | collective-permute-start | bytes 12296 | tf_op jit(solution)/shard_map/ppermute | solution.py:163
  173.1 9.6 %collective-permute-start.59 = (bf16[1,8,256]{2,1,0:T(8,128)(2,1)S(1)}, bf16[1,8,256]{2,1,0:T(8,128)(2,1)S(1)}, u32[]{:S(2)}, u32[]{:S(2)}) collective-permute-start(bf16[1,8,256]{2,1,0:T(8,128)(2,1)S(1)} %get-tuple-element.143), channel_id=1, source_target_pairs={{0,4},{2,6},{4,0},{6,2},{8,12},{10,14},{12,8},{14,10},{1,5},{3,7},... | collective-permute-start | bytes 12296 | tf_op jit(solution)/shard_map/ppermute | solution.py:163
  173.2 10.7 %collective-permute-start.60 = (bf16[1,8,256]{2,1,0:T(8,128)(2,1)S(1)}, bf16[1,8,256]{2,1,0:T(8,128)(2,1)S(1)}, u32[]{:S(2)}, u32[]{:S(2)}) collective-permute-start(bf16[1,8,256]{2,1,0:T(8,128)(2,1)S(1)} %get-tuple-element.142), channel_id=1, source_target_pairs={{0,6},{2,4},{4,2},{6,0},{8,14},{10,12},{12,10},{14,8},{1,7},{3,5},... | collective-permute-start | bytes 12296 | tf_op jit(solution)/shard_map/ppermute | solution.py:163
  183.9 14.2 %collective-permute-start.51 = (bf16[1,16,512]{2,1,0:T(8,128)(2,1)}, bf16[1,16,512]{2,1,0:T(8,128)(2,1)}, u32[]{:S(2)}, u32[]{:S(2)}) collective-permute-start(bf16[1,16,512]{2,1,0:T(8,128)(2,1)} %get-tuple-element.91), channel_id=1, source_target_pairs={{0,2},{2,0},{4,6},{6,4},{8,10},{10,8},{12,14},{14,12},{1,3},{3,1},... | collective-permute-start | bytes 49160 | tf_op jit(solution)/shard_map/ppermute | solution.py:163
  184.3 18.8 %collective-permute-start.52 = (bf16[1,16,512]{2,1,0:T(8,128)(2,1)}, bf16[1,16,512]{2,1,0:T(8,128)(2,1)}, u32[]{:S(2)}, u32[]{:S(2)}) collective-permute-start(bf16[1,16,512]{2,1,0:T(8,128)(2,1)} %get-tuple-element.90), channel_id=1, source_target_pairs={{0,4},{2,6},{4,0},{6,2},{8,12},{10,14},{12,8},{14,10},{1,5},{3,7},... | collective-permute-start | bytes 49160 | tf_op jit(solution)/shard_map/ppermute | solution.py:163
  184.4 21.2 %collective-permute-start.53 = (bf16[1,16,512]{2,1,0:T(8,128)(2,1)}, bf16[1,16,512]{2,1,0:T(8,128)(2,1)}, u32[]{:S(2)}, u32[]{:S(2)}) collective-permute-start(bf16[1,16,512]{2,1,0:T(8,128)(2,1)} %get-tuple-element.89), channel_id=1, source_target_pairs={{0,6},{2,4},{4,2},{6,0},{8,14},{10,12},{12,10},{14,8},{1,7},{3,5},... | collective-permute-start | bytes 49160 | tf_op jit(solution)/shard_map/ppermute | solution.py:163
  187.4 19.9 %collective-permute-start.54 = (bf16[1,16,512]{2,1,0:T(8,128)(2,1)}, bf16[1,16,512]{2,1,0:T(8,128)(2,1)}, u32[]{:S(2)}, u32[]{:S(2)}) collective-permute-start(bf16[1,16,512]{2,1,0:T(8,128)(2,1)} %get-tuple-element.88), channel_id=1, source_target_pairs={{0,8},{2,10},{4,12},{6,14},{8,0},{10,2},{12,4},{14,6},{1,9},{3,11}... | collective-permute-start | bytes 49160 | tf_op jit(solution)/shard_map/ppermute | solution.py:163
  190.0 18.7 %collective-permute-start.55 = (bf16[1,16,512]{2,1,0:T(8,128)(2,1)}, bf16[1,16,512]{2,1,0:T(8,128)(2,1)}, u32[]{:S(2)}, u32[]{:S(2)}) collective-permute-start(bf16[1,16,512]{2,1,0:T(8,128)(2,1)} %get-tuple-element.87), channel_id=1, source_target_pairs={{0,10},{2,8},{4,14},{6,12},{8,2},{10,0},{12,6},{14,4},{1,11},{3,9}... | collective-permute-start | bytes 49160 | tf_op jit(solution)/shard_map/ppermute | solution.py:163
  198.1 15.0 %collective-permute-start.56 = (bf16[1,16,512]{2,1,0:T(8,128)(2,1)}, bf16[1,16,512]{2,1,0:T(8,128)(2,1)S(1)}, u32[]{:S(2)}, u32[]{:S(2)}) collective-permute-start(bf16[1,16,512]{2,1,0:T(8,128)(2,1)} %get-tuple-element.86), channel_id=1, source_target_pairs={{0,12},{2,14},{4,8},{6,10},{8,4},{10,6},{12,0},{14,2},{1,13},{3,15... | collective-permute-start | bytes 49160 | tf_op jit(solution)/shard_map/ppermute | solution.py:163
  203.1 12.7 %collective-permute-start.57 = (bf16[1,16,512]{2,1,0:T(8,128)(2,1)}, bf16[1,16,512]{2,1,0:T(8,128)(2,1)S(1)}, u32[]{:S(2)}, u32[]{:S(2)}) collective-permute-start(bf16[1,16,512]{2,1,0:T(8,128)(2,1)} %get-tuple-element.85), channel_id=1, source_target_pairs={{0,14},{2,12},{4,10},{6,8},{8,6},{10,4},{12,2},{14,0},{1,15},{3,13... | collective-permute-start | bytes 49160 | tf_op jit(solution)/shard_map/ppermute | solution.py:163
  205.6 11.5 %collective-permute-start.44 = (bf16[1,16,512]{2,1,0:T(8,128)(2,1)}, bf16[1,16,512]{2,1,0:T(8,128)(2,1)S(1)}, u32[]{:S(2)}, u32[]{:S(2)}) collective-permute-start(bf16[1,16,512]{2,1,0:T(8,128)(2,1)} %get-tuple-element.99), channel_id=1, source_target_pairs={{0,2},{2,0},{4,6},{6,4},{8,10},{10,8},{12,14},{14,12},{1,3},{3,1},... | collective-permute-start | bytes 49160 | tf_op jit(solution)/shard_map/ppermute | solution.py:163
  207.3 13.4 %collective-permute-start.45 = (bf16[1,16,512]{2,1,0:T(8,128)(2,1)}, bf16[1,16,512]{2,1,0:T(8,128)(2,1)S(1)}, u32[]{:S(2)}, u32[]{:S(2)}) collective-permute-start(bf16[1,16,512]{2,1,0:T(8,128)(2,1)} %get-tuple-element.98), channel_id=1, source_target_pairs={{0,4},{2,6},{4,0},{6,2},{8,12},{10,14},{12,8},{14,10},{1,5},{3,7},... | collective-permute-start | bytes 49160 | tf_op jit(solution)/shard_map/ppermute | solution.py:163
  208.7 13.3 %collective-permute-start.46 = (bf16[1,16,512]{2,1,0:T(8,128)(2,1)}, bf16[1,16,512]{2,1,0:T(8,128)(2,1)S(1)}, u32[]{:S(2)}, u32[]{:S(2)}) collective-permute-start(bf16[1,16,512]{2,1,0:T(8,128)(2,1)} %get-tuple-element.97), channel_id=1, source_target_pairs={{0,6},{2,4},{4,2},{6,0},{8,14},{10,12},{12,10},{14,8},{1,7},{3,5},... | collective-permute-start | bytes 49160 | tf_op jit(solution)/shard_map/ppermute | solution.py:163
  213.0 9.5 %collective-permute-start.47 = (bf16[1,16,512]{2,1,0:T(8,128)(2,1)}, bf16[1,16,512]{2,1,0:T(8,128)(2,1)S(1)}, u32[]{:S(2)}, u32[]{:S(2)}) collective-permute-start(bf16[1,16,512]{2,1,0:T(8,128)(2,1)} %get-tuple-element.96), channel_id=1, source_target_pairs={{0,8},{2,10},{4,12},{6,14},{8,0},{10,2},{12,4},{14,6},{1,9},{3,11}... | collective-permute-start | bytes 49160 | tf_op jit(solution)/shard_map/ppermute | solution.py:163
  222.5 9.9 %collective-permute-start.38 = (bf16[1,16,512]{2,1,0:T(8,128)(2,1)S(1)}, bf16[1,16,512]{2,1,0:T(8,128)(2,1)S(1)}, u32[]{:S(2)}, u32[]{:S(2)}) collective-permute-start(bf16[1,16,512]{2,1,0:T(8,128)(2,1)S(1)} %copy-done.44), channel_id=1, source_target_pairs={{0,4},{2,6},{4,0},{6,2},{8,12},{10,14},{12,8},{14,10},{1,5},{3,7},... | collective-permute-start | bytes 49160 | tf_op jit(solution)/shard_map/ppermute | solution.py:163
  222.6 11.1 %collective-permute-start.39 = (bf16[1,16,512]{2,1,0:T(8,128)(2,1)S(1)}, bf16[1,16,512]{2,1,0:T(8,128)(2,1)S(1)}, u32[]{:S(2)}, u32[]{:S(2)}) collective-permute-start(bf16[1,16,512]{2,1,0:T(8,128)(2,1)S(1)} %copy-done.43), channel_id=1, source_target_pairs={{0,6},{2,4},{4,2},{6,0},{8,14},{10,12},{12,10},{14,8},{1,7},{3,5},... | collective-permute-start | bytes 49160 | tf_op jit(solution)/shard_map/ppermute | solution.py:163
  234.2 10.5 %collective-permute-start.31 = (bf16[1,16,512]{2,1,0:T(8,128)(2,1)S(1)}, bf16[1,16,512]{2,1,0:T(8,128)(2,1)S(1)}, u32[]{:S(2)}, u32[]{:S(2)}) collective-permute-start(bf16[1,16,512]{2,1,0:T(8,128)(2,1)S(1)} %copy-done.37), channel_id=1, source_target_pairs={{0,4},{2,6},{4,0},{6,2},{8,12},{10,14},{12,8},{14,10},{1,5},{3,7},... | collective-permute-start | bytes 49160 | tf_op jit(solution)/shard_map/ppermute | solution.py:163
  234.3 12.2 %collective-permute-start.32 = (bf16[1,16,512]{2,1,0:T(8,128)(2,1)S(1)}, bf16[1,16,512]{2,1,0:T(8,128)(2,1)S(1)}, u32[]{:S(2)}, u32[]{:S(2)}) collective-permute-start(bf16[1,16,512]{2,1,0:T(8,128)(2,1)S(1)} %copy-done.36), channel_id=1, source_target_pairs={{0,6},{2,4},{4,2},{6,0},{8,14},{10,12},{12,10},{14,8},{1,7},{3,5},... | collective-permute-start | bytes 49160 | tf_op jit(solution)/shard_map/ppermute | solution.py:163
  237.4 10.1 %collective-permute-start.33 = (bf16[1,16,512]{2,1,0:T(8,128)(2,1)S(1)}, bf16[1,16,512]{2,1,0:T(8,128)(2,1)S(1)}, u32[]{:S(2)}, u32[]{:S(2)}) collective-permute-start(bf16[1,16,512]{2,1,0:T(8,128)(2,1)S(1)} %copy-done.35), channel_id=1, source_target_pairs={{0,8},{2,10},{4,12},{6,14},{8,0},{10,2},{12,4},{14,6},{1,9},{3,11}... | collective-permute-start | bytes 49160 | tf_op jit(solution)/shard_map/ppermute | solution.py:163
  240.4 11.4 %collective-permute-start.35 = (bf16[1,16,512]{2,1,0:T(8,128)(2,1)S(1)}, bf16[1,16,512]{2,1,0:T(8,128)(2,1)S(1)}, u32[]{:S(2)}, u32[]{:S(2)}) collective-permute-start(bf16[1,16,512]{2,1,0:T(8,128)(2,1)S(1)} %copy-done.33), channel_id=1, source_target_pairs={{0,12},{2,14},{4,8},{6,10},{8,4},{10,6},{12,0},{14,2},{1,13},{3,15... | collective-permute-start | bytes 49160 | tf_op jit(solution)/shard_map/ppermute | solution.py:163
  244.7 13.8 %collective-permute-start.36 = (bf16[1,16,512]{2,1,0:T(8,128)(2,1)S(1)}, bf16[1,16,512]{2,1,0:T(8,128)(2,1)}, u32[]{:S(2)}, u32[]{:S(2)}) collective-permute-start(bf16[1,16,512]{2,1,0:T(8,128)(2,1)S(1)} %get-tuple-element.109), channel_id=1, source_target_pairs={{0,14},{2,12},{4,10},{6,8},{8,6},{10,4},{12,2},{14,0},{1,15},{3,13... | collective-permute-start | bytes 49160 | tf_op jit(solution)/shard_map/ppermute | solution.py:163
  246.5 24.8 %collective-permute-start.23 = (bf16[1,32,1024]{2,1,0:T(8,128)(2,1)}, bf16[1,32,1024]{2,1,0:T(8,128)(2,1)S(1)}, u32[]{:S(2)}, u32[]{:S(2)}) collective-permute-start(bf16[1,32,1024]{2,1,0:T(8,128)(2,1)} %get-tuple-element.51), channel_id=1, source_target_pairs={{0,2},{2,0},{4,6},{6,4},{8,10},{10,8},{12,14},{14,12},{1,3},{3,1},... | collective-permute-start | bytes 196616 | tf_op jit(solution)/shard_map/ppermute | solution.py:163
  247.5 27.5 %collective-permute-start.24 = (bf16[1,32,1024]{2,1,0:T(8,128)(2,1)}, bf16[1,32,1024]{2,1,0:T(8,128)(2,1)}, u32[]{:S(2)}, u32[]{:S(2)}) collective-permute-start(bf16[1,32,1024]{2,1,0:T(8,128)(2,1)} %get-tuple-element.50), channel_id=1, source_target_pairs={{0,4},{2,6},{4,0},{6,2},{8,12},{10,14},{12,8},{14,10},{1,5},{3,7},... | collective-permute-start | bytes 196616 | tf_op jit(solution)/shard_map/ppermute | solution.py:163
  248.1 29.0 %collective-permute-start.25 = (bf16[1,32,1024]{2,1,0:T(8,128)(2,1)}, bf16[1,32,1024]{2,1,0:T(8,128)(2,1)}, u32[]{:S(2)}, u32[]{:S(2)}) collective-permute-start(bf16[1,32,1024]{2,1,0:T(8,128)(2,1)} %get-tuple-element.49), channel_id=1, source_target_pairs={{0,6},{2,4},{4,2},{6,0},{8,14},{10,12},{12,10},{14,8},{1,7},{3,5},... | collective-permute-start | bytes 196616 | tf_op jit(solution)/shard_map/ppermute | solution.py:163
  251.8 26.6 %collective-permute-start.26 = (bf16[1,32,1024]{2,1,0:T(8,128)(2,1)}, bf16[1,32,1024]{2,1,0:T(8,128)(2,1)}, u32[]{:S(2)}, u32[]{:S(2)}) collective-permute-start(bf16[1,32,1024]{2,1,0:T(8,128)(2,1)} %get-tuple-element.48), channel_id=1, source_target_pairs={{0,8},{2,10},{4,12},{6,14},{8,0},{10,2},{12,4},{14,6},{1,9},{3,11}... | collective-permute-start | bytes 196616 | tf_op jit(solution)/shard_map/ppermute | solution.py:163
  258.6 20.8 %collective-permute-start.27 = (bf16[1,32,1024]{2,1,0:T(8,128)(2,1)}, bf16[1,32,1024]{2,1,0:T(8,128)(2,1)}, u32[]{:S(2)}, u32[]{:S(2)}) collective-permute-start(bf16[1,32,1024]{2,1,0:T(8,128)(2,1)} %get-tuple-element.47), channel_id=1, source_target_pairs={{0,10},{2,8},{4,14},{6,12},{8,2},{10,0},{12,6},{14,4},{1,11},{3,9}... | collective-permute-start | bytes 196616 | tf_op jit(solution)/shard_map/ppermute | solution.py:163
  271.3 12.1 %collective-permute-start.28 = (bf16[1,32,1024]{2,1,0:T(8,128)(2,1)}, bf16[1,32,1024]{2,1,0:T(8,128)(2,1)S(1)}, u32[]{:S(2)}, u32[]{:S(2)}) collective-permute-start(bf16[1,32,1024]{2,1,0:T(8,128)(2,1)} %get-tuple-element.46), channel_id=1, source_target_pairs={{0,12},{2,14},{4,8},{6,10},{8,4},{10,6},{12,0},{14,2},{1,13},{3,15... | collective-permute-start | bytes 196616 | tf_op jit(solution)/shard_map/ppermute | solution.py:163
  275.0 10.6 %collective-permute-start.29 = (bf16[1,32,1024]{2,1,0:T(8,128)(2,1)}, bf16[1,32,1024]{2,1,0:T(8,128)(2,1)S(1)}, u32[]{:S(2)}, u32[]{:S(2)}) collective-permute-start(bf16[1,32,1024]{2,1,0:T(8,128)(2,1)} %get-tuple-element.45), channel_id=1, source_target_pairs={{0,14},{2,12},{4,10},{6,8},{8,6},{10,4},{12,2},{14,0},{1,15},{3,13... | collective-permute-start | bytes 196616 | tf_op jit(solution)/shard_map/ppermute | solution.py:163
  278.5 11.8 %collective-permute-start.17 = (bf16[1,32,1024]{2,1,0:T(8,128)(2,1)}, bf16[1,32,1024]{2,1,0:T(8,128)(2,1)S(1)}, u32[]{:S(2)}, u32[]{:S(2)}) collective-permute-start(bf16[1,32,1024]{2,1,0:T(8,128)(2,1)} %get-tuple-element.58), channel_id=1, source_target_pairs={{0,4},{2,6},{4,0},{6,2},{8,12},{10,14},{12,8},{14,10},{1,5},{3,7},... | collective-permute-start | bytes 196616 | tf_op jit(solution)/shard_map/ppermute | solution.py:163
  279.4 12.1 %collective-permute-start.18 = (bf16[1,32,1024]{2,1,0:T(8,128)(2,1)}, bf16[1,32,1024]{2,1,0:T(8,128)(2,1)S(1)}, u32[]{:S(2)}, u32[]{:S(2)}) collective-permute-start(bf16[1,32,1024]{2,1,0:T(8,128)(2,1)} %get-tuple-element.57), channel_id=1, source_target_pairs={{0,6},{2,4},{4,2},{6,0},{8,14},{10,12},{12,10},{14,8},{1,7},{3,5},... | collective-permute-start | bytes 196616 | tf_op jit(solution)/shard_map/ppermute | solution.py:163
  285.7 10.3 %collective-permute-start.20 = (bf16[1,32,1024]{2,1,0:T(8,128)(2,1)S(1)}, bf16[1,32,1024]{2,1,0:T(8,128)(2,1)S(1)}, u32[]{:S(2)}, u32[]{:S(2)}) collective-permute-start(bf16[1,32,1024]{2,1,0:T(8,128)(2,1)S(1)} %copy-done.32), channel_id=1, source_target_pairs={{0,10},{2,8},{4,14},{6,12},{8,2},{10,0},{12,6},{14,4},{1,11},{3,9}... | collective-permute-start | bytes 196616 | tf_op jit(solution)/shard_map/ppermute | solution.py:163
  286.5 9.6 %collective-permute-start.21 = (bf16[1,32,1024]{2,1,0:T(8,128)(2,1)S(1)}, bf16[1,32,1024]{2,1,0:T(8,128)(2,1)S(1)}, u32[]{:S(2)}, u32[]{:S(2)}) collective-permute-start(bf16[1,32,1024]{2,1,0:T(8,128)(2,1)S(1)} %copy-done.31), channel_id=1, source_target_pairs={{0,12},{2,14},{4,8},{6,10},{8,4},{10,6},{12,0},{14,2},{1,13},{3,15... | collective-permute-start | bytes 196616 | tf_op jit(solution)/shard_map/ppermute | solution.py:163
  290.3 10.7 %collective-permute-start.22 = (bf16[1,32,1024]{2,1,0:T(8,128)(2,1)S(1)}, bf16[1,32,1024]{2,1,0:T(8,128)(2,1)S(1)}, u32[]{:S(2)}, u32[]{:S(2)}) collective-permute-start(bf16[1,32,1024]{2,1,0:T(8,128)(2,1)S(1)} %copy-done.30), channel_id=1, source_target_pairs={{0,14},{2,12},{4,10},{6,8},{8,6},{10,4},{12,2},{14,0},{1,15},{3,13... | collective-permute-start | bytes 196616 | tf_op jit(solution)/shard_map/ppermute | solution.py:163
  291.6 10.5 %collective-permute-start.9 = (bf16[1,32,1024]{2,1,0:T(8,128)(2,1)S(1)}, bf16[1,32,1024]{2,1,0:T(8,128)(2,1)S(1)}, u32[]{:S(2)}, u32[]{:S(2)}) collective-permute-start(bf16[1,32,1024]{2,1,0:T(8,128)(2,1)S(1)} %copy-done.29), channel_id=1, source_target_pairs={{0,2},{2,0},{4,6},{6,4},{8,10},{10,8},{12,14},{14,12},{1,3},{3,1},... | collective-permute-start | bytes 196616 | tf_op jit(solution)/shard_map/ppermute | solution.py:163
  292.1 12.3 %collective-permute-start.10 = (bf16[1,32,1024]{2,1,0:T(8,128)(2,1)S(1)}, bf16[1,32,1024]{2,1,0:T(8,128)(2,1)S(1)}, u32[]{:S(2)}, u32[]{:S(2)}) collective-permute-start(bf16[1,32,1024]{2,1,0:T(8,128)(2,1)S(1)} %copy-done.28), channel_id=1, source_target_pairs={{0,4},{2,6},{4,0},{6,2},{8,12},{10,14},{12,8},{14,10},{1,5},{3,7},... | collective-permute-start | bytes 196616 | tf_op jit(solution)/shard_map/ppermute | solution.py:163
  295.9 10.3 %collective-permute-start.11 = (bf16[1,32,1024]{2,1,0:T(8,128)(2,1)S(1)}, bf16[1,32,1024]{2,1,0:T(8,128)(2,1)S(1)}, u32[]{:S(2)}, u32[]{:S(2)}) collective-permute-start(bf16[1,32,1024]{2,1,0:T(8,128)(2,1)S(1)} %copy-done.27), channel_id=1, source_target_pairs={{0,6},{2,4},{4,2},{6,0},{8,14},{10,12},{12,10},{14,8},{1,7},{3,5},... | collective-permute-start | bytes 196616 | tf_op jit(solution)/shard_map/ppermute | solution.py:163
  296.1 11.5 %collective-permute-start.12 = (bf16[1,32,1024]{2,1,0:T(8,128)(2,1)S(1)}, bf16[1,32,1024]{2,1,0:T(8,128)(2,1)S(1)}, u32[]{:S(2)}, u32[]{:S(2)}) collective-permute-start(bf16[1,32,1024]{2,1,0:T(8,128)(2,1)S(1)} %copy-done.26), channel_id=1, source_target_pairs={{0,8},{2,10},{4,12},{6,14},{8,0},{10,2},{12,4},{14,6},{1,9},{3,11}... | collective-permute-start | bytes 196616 | tf_op jit(solution)/shard_map/ppermute | solution.py:163
  307.8 10.3 %collective-permute-start.4 = (bf16[1,32,1024]{2,1,0:T(8,128)(2,1)S(1)}, bf16[1,32,1024]{2,1,0:T(8,128)(2,1)S(1)}, u32[]{:S(2)}, u32[]{:S(2)}) collective-permute-start(bf16[1,32,1024]{2,1,0:T(8,128)(2,1)S(1)} %copy-done.20), channel_id=1, source_target_pairs={{0,6},{2,4},{4,2},{6,0},{8,14},{10,12},{12,10},{14,8},{1,7},{3,5},... | collective-permute-start | bytes 196616 | tf_op jit(solution)/shard_map/ppermute | solution.py:163
  (87 other events, 1158.4 us)
